TPU v7x, 256 devices: a whole 4x4x8 slice. The times are simulated.
256 devices in a mesh: seq: 64 (over x, z, core), ch: 4 (over y).
Axes of the slice: x: 4, y: 4, z: 8, core: 2. Of those that a mesh axis runs over, the one named last changes fastest.
Arguments:
- inputs: bfloat16 [8192, 4096], P('seq'), may hold values from -6 to 6
- norm_gain: float32 [4096], replicated, may hold values from 0.1 to 1.9
- in_weight: bfloat16 [4096, 3, 1024], P('seq', None, 'ch'), may hold values from -0.09375 to 0.09375
- short_filter: float32 [3, 3, 1024], P(None, None, 'ch'), may hold values from -4 to 4
- long_filter: float32 [8192, 1024], P('seq', 'ch'), may hold values from -2.2 to 2.2
- conv_bias: float32 [1024], P('ch'), may hold values from -4 to 4
- out_weight: bfloat16 [1024, 4096], P('ch', 'seq'), may hold values from -0.1875 to 0.1875
- out_grad: bfloat16 [8192, 4096], P('seq'), may hold values from -6 to 6
Outputs:
- block_out: bfloat16 [8192, 4096], P('seq', 'ch')
- in_grad: bfloat16 [8192, 4096], P('seq')
- filter_grad: float32 [8192, 1024], P('seq', 'ch')
All inputs are finite; a program needn't handle non-finite values.
Results may differ from a plain program's by a relative error of at most 0.013.
Values may be sent and summed in bfloat16 or wider, within the bound.
No kernel may reach another device: no remote copies, remote signals or barrier semaphores. Data moves between devices by JAX's collectives and lax.ppermute only.
A program may use at most 64 MiB of HBM per device.

v0:
```python
import math
import jax
import jax.numpy as jnp
from jax import lax
from jax.sharding import PartitionSpec as P

epsilon = 1e-05
highest = lax.Precision.HIGHEST


def passed_along(block, axis, distance):
    devices = range(lax.axis_size(axis))
    route = [(i - distance, i) for i in devices if i - distance in devices]
    return lax.ppermute(block, axis, route)


def to_columns(signals):
    return lax.all_to_all(signals, "seq", split_axis=1, concat_axis=2, tiled=True)


def to_rows(signals):
    return lax.all_to_all(signals, "seq", split_axis=2, concat_axis=1, tiled=True)


def turn_table(rows, cols, period, sign):
    turns = jnp.arange(rows, dtype=jnp.int32)[:, None] * jnp.arange(cols, dtype=jnp.int32)[None, :]
    phases = sign * 2.0 * math.pi / period * (turns % period).astype(jnp.float32)
    return (jnp.cos(phases), jnp.sin(phases))


def fft_sizes(seq_total):
    total = 2 * seq_total
    inner = 1
    while inner * inner < total:
        inner *= 2
    return (total // inner, inner)


def forward_dft(signals):
    count, chans, seq_total = signals.shape
    outer, inner = fft_sizes(seq_total)
    grid = signals.reshape(count, chans, outer // 2, inner)
    cos_out, sin_out = turn_table(outer, outer // 2, outer, 1.0)
    first_real = jnp.einsum("kn,ucnm->uckm", cos_out, grid, precision=highest)
    first_imag = -jnp.einsum("kn,ucnm->uckm", sin_out, grid, precision=highest)
    cos_tw, sin_tw = turn_table(outer, inner, outer * inner, 1.0)
    turned_real = first_real * cos_tw + first_imag * sin_tw
    turned_imag = first_imag * cos_tw - first_real * sin_tw
    cos_in, sin_in = turn_table(inner, inner, inner, 1.0)
    spec_real = jnp.einsum("uckm,mj->uckj", turned_real, cos_in, precision=highest) + jnp.einsum(
        "uckm,mj->uckj", turned_imag, sin_in, precision=highest
    )
    spec_imag = jnp.einsum("uckm,mj->uckj", turned_imag, cos_in, precision=highest) - jnp.einsum(
        "uckm,mj->uckj", turned_real, sin_in, precision=highest
    )
    return (spec_real, spec_imag)


def inverse_dft(spec_real, spec_imag):
    count, chans, outer, inner = spec_real.shape
    cos_in, sin_in = turn_table(inner, inner, inner, 1.0)
    back_real = jnp.einsum("uckj,jm->uckm", spec_real, cos_in, precision=highest) - jnp.einsum(
        "uckj,jm->uckm", spec_imag, sin_in, precision=highest
    )
    back_imag = jnp.einsum("uckj,jm->uckm", spec_imag, cos_in, precision=highest) + jnp.einsum(
        "uckj,jm->uckm", spec_real, sin_in, precision=highest
    )
    cos_tw, sin_tw = turn_table(outer, inner, outer * inner, 1.0)
    turned_real = back_real * cos_tw - back_imag * sin_tw
    turned_imag = back_imag * cos_tw + back_real * sin_tw
    cos_out, sin_out = turn_table(outer, outer // 2, outer, 1.0)
    grid = jnp.einsum("kn,uckm->ucnm", cos_out, turned_real, precision=highest) - jnp.einsum(
        "kn,uckm->ucnm", sin_out, turned_imag, precision=highest
    )
    return grid.reshape(count, chans, outer * inner // 2) / float(outer * inner)


def per_device(
    inputs, norm_gain, in_weight, short_filter, long_filter, conv_bias, out_weight, out_grad
):
    local_rows = inputs.shape[0]
    model_width = inputs.shape[1]
    slab_width = long_filter.shape[1]
    taps = short_filter.shape[1]
    wide_inputs = inputs.astype(jnp.float32)
    inv_rms = lax.rsqrt(jnp.mean(wide_inputs * wide_inputs, axis=1, keepdims=True) + epsilon)
    normed = (wide_inputs * inv_rms * norm_gain).astype(jnp.bfloat16)
    in_panel, out_panel = (
        lax.all_gather(in_weight, "seq", axis=0, tiled=True),
        lax.all_gather(out_weight, "seq", axis=1, tiled=True),
    )
    in_flat = in_panel.reshape(model_width, 3 * slab_width)
    projected = jnp.dot(normed, in_flat, preferred_element_type=jnp.float32)
    projected = projected.astype(jnp.bfloat16).reshape(local_rows, 3, slab_width)
    upper_rim = passed_along(projected[local_rows - (taps - 1) :], "seq", 1)
    extended = jnp.concatenate([upper_rim, projected], 0).astype(jnp.float32)
    mixed = jnp.zeros((local_rows, 3, slab_width), jnp.float32)
    for offset in range(taps):
        begin = taps - 1 - offset
        mixed = mixed + short_filter[:, offset, :][None] * extended[begin : begin + local_rows]
    query_br = mixed[:, 0]
    key_br = mixed[:, 1]
    value_br = mixed[:, 2]
    product = key_br * value_br
    gate_grad = jnp.dot(out_grad, out_panel.T, preferred_element_type=jnp.float32)
    carried = gate_grad * query_br
    columns = to_columns(jnp.stack([product, long_filter, carried]).transpose(0, 2, 1))
    all_real, all_imag = forward_dft(columns)
    sig_real, filt_real, grad_real = (all_real[0], all_real[1], all_real[2])
    sig_imag, filt_imag, grad_imag = (all_imag[0], all_imag[1], all_imag[2])
    conv_real = sig_real * filt_real - sig_imag * filt_imag
    conv_imag = sig_real * filt_imag + sig_imag * filt_real
    back_real = grad_real * filt_real + grad_imag * filt_imag
    back_imag = grad_imag * filt_real - grad_real * filt_imag
    pair_real = grad_real * sig_real + grad_imag * sig_imag
    pair_imag = grad_imag * sig_real - grad_real * sig_imag
    outs = inverse_dft(
        jnp.stack([conv_real, back_real, pair_real]), jnp.stack([conv_imag, back_imag, pair_imag])
    )
    returned = to_rows(outs).transpose(0, 2, 1)
    conv_out = returned[0]
    back_conv = returned[1]
    filter_grad = returned[2] * float(local_rows * lax.axis_size("seq")) ** (-0.5)
    biased = conv_out + conv_bias * product
    gated = (query_br * biased).astype(jnp.bfloat16)
    partial_out = jnp.dot(gated, out_panel, preferred_element_type=jnp.float32)
    summed = lax.psum_scatter(
        partial_out.astype(jnp.bfloat16), "ch", scatter_dimension=1, tiled=True
    ).astype(jnp.float32)
    share = summed.shape[1]
    residual = lax.dynamic_slice_in_dim(wide_inputs, lax.axis_index("ch") * share, share, 1)
    block_out = (residual + summed).astype(jnp.bfloat16)
    source_grad = back_conv + conv_bias * carried
    mixed_grad = jnp.stack([gate_grad * biased, source_grad * value_br, source_grad * key_br], 1)
    lower_rim = passed_along(mixed_grad[: taps - 1], "seq", -1)
    extended_back = jnp.concatenate([mixed_grad, lower_rim], 0)
    proj_grad = jnp.zeros((local_rows, 3, slab_width), jnp.float32)
    for offset in range(taps):
        proj_grad = (
            proj_grad
            + short_filter[:, offset, :][None] * extended_back[offset : offset + local_rows]
        )
    proj_grad = proj_grad.astype(jnp.bfloat16).reshape(local_rows, 3 * slab_width)
    partial_grad = jnp.dot(proj_grad, in_flat.T, preferred_element_type=jnp.float32)
    norm_grad = lax.psum(partial_grad, "ch")
    weighted = norm_grad * norm_gain
    inner_term = jnp.mean(weighted * wide_inputs, axis=1, keepdims=True)
    in_grad = (
        out_grad.astype(jnp.float32) + weighted * inv_rms - wide_inputs * inv_rms**3 * inner_term
    ).astype(jnp.bfloat16)
    return (block_out, in_grad, filter_grad)


def solution(mesh):
    return jax.shard_map(
        per_device,
        mesh=mesh,
        in_specs=(
            P("seq", None),
            P(),
            P("seq", None, "ch"),
            P(None, None, "ch"),
            P("seq", "ch"),
            P("ch"),
            P("ch", "seq"),
            P("seq", None),
        ),
        out_specs=(P("seq", "ch"), P("seq", None), P("seq", "ch")),
        check_vma=False,
    )
```

profile of v0, /device:TPU:1, one launch (start us, length us, event | category | flops | bytes accessed | tf_op | source)
XLA Modules:
  0.0 393.4 jit_solution(6677568835043596494)
XLA Ops:
  7.2 0.7 all-gather.3.cloned.1.call-update
  7.9 0.7 all-gather.5.cloned.1.call-update
  8.6 0.8 fusion.142
  9.5 1.5 multiply_reduce_fusion.1
  11.0 0.6 multiply_multiply_fusion
  11.6 83.9 %all-gather.3.cloned.1.call-done = bf16[4096,3,256]{2,0,1:T(8,128)(2,1)} async-done(((bf16[64,3,256]{2,0,1:T(8,128)(2,1)}), bf16[4096,3,256]{2,0,1:T(8,128)(2,1)}) %all-gather.3.cloned.1.call-update) | async-done | bytes 6291472 | tf_op jit(solution)/shard_map/all_gather | solution.py:89
  95.5 8.7 %copy.46 = bf16[4096,3,256]{0,2,1:T(8,128)(2,1)} copy(bf16[4096,3,256]{2,0,1:T(8,128)(2,1)} %all-gather.3.cloned.1.call-done) | data formatting | bytes 12582912 | tf_op jit(solution)/shard_map/all_gather | solution.py:89
  104.2 5.1 %convolution_convert_fusion.1 = bf16[128,768]{1,0:T(8,128)(2,1)S(1)} fusion(bf16[4096,768]{0,1:T(8,128)(2,1)} %bitcast.127, bf16[128,4096]{1,0:T(8,128)(2,1)S(1)} %copy-done, f32[4096]{0:T(1024)S(1)} %copy-done.9, f32[128]{0:T(128)S(1)} %get-tuple-element.19), kind=kOutput, calls=%fused_computation.16 | convolution fusion | flops 807501824 | bytes 7553536 | tf_op jit(solution)/shard_map/dot_general | solution.py:93
  109.3 2.7 collective-permute-start
  112.1 60.2 %all-gather.5.cloned.1.call-done = bf16[256,4096]{0,1:T(8,128)(2,1)} async-done(((bf16[256,64]{0,1:T(8,128)(2,1)}), bf16[256,4096]{0,1:T(8,128)(2,1)}) %all-gather.5.cloned.1.call-update) | async-done | bytes 2097168 | tf_op jit(solution)/shard_map/all_gather | solution.py:90
  172.3 2.0 fusion.143
  175.4 1.0 copy.50
  176.4 6.6 %all-to-all-start = ((f32[3,256,128]{2,0,1:T(4,128)}), f32[3,256,128]{2,0,1:T(4,128)S(1)}, u32[]{:S(2)}, u32[]{:S(2)}) async-start(f32[3,256,128]{2,0,1:T(4,128)} %copy.50), calls=%async_computation | async-start | bytes 1048576 | tf_op jit(solution)/shard_map/all_to_all | solution.py:18
  183.9 16.3 %all-to-all-done = f32[3,256,128]{2,0,1:T(4,128)S(1)} async-done(((f32[3,256,128]{2,0,1:T(4,128)}), f32[3,256,128]{2,0,1:T(4,128)S(1)}, u32[]{:S(2)}, u32[]{:S(2)}) %all-to-all-start) | async-done | bytes 393248 | tf_op jit(solution)/shard_map/all_to_all | solution.py:18
  200.3 1.5 convolution_bitcast_fusion.1
  201.8 1.5 fusion
  203.3 1.6 fusion.31
  204.9 1.6 fusion.32
  206.5 1.6 convolution_add_fusion.1
  208.1 1.6 convolution_subtract_fusion.1
  209.9 1.1 fusion.13
  211.0 1.3 fusion.12
  212.4 1.1 convolution_subtract_fusion
  213.5 1.1 convolution_add_fusion
  214.6 1.2 fusion.8
  215.8 1.2 fusion.2
  217.0 8.6 %copy.85 = f32[3,4,64,128]{1,0,3,2:T(4,128)} copy(f32[3,4,64,128]{3,2,1,0:T(8,128)S(1)} %fusion.2) | data formatting | bytes 786432 | tf_op jit(solution)/shard_map/div | solution.py:75
  225.6 16.0 %reshape.105 = f32[64,1,1536]{2,1,0:T(1,128)S(1)} reshape(f32[8192,3,4]{2,1,0:T(4,128)} %bitcast.125) | data formatting | bytes 786432
  241.6 20.6 %all_to_all.33 = f32[64,1,1536]{2,1,0:T(1,128)S(1)} all-to-all(f32[64,1,1536]{2,1,0:T(1,128)S(1)} %reshape.105), channel_id=1, replica_groups=mesh['seq'=64,'ch'=4] {'seq'}, dimensions={0} | all-to-all | bytes 786432 | tf_op jit(solution)/shard_map/all_to_all | solution.py:22
  262.8 1.6 reduce
  264.4 11.6 %reshape.106 = f32[8192,3,4]{2,1,0:T(4,128)} reshape(f32[64,1536]{1,0:T(8,128)S(1)} %reduce) | data formatting | bytes 786432
  275.9 10.1 %copy.86 = f32[3,4,64,128]{3,2,1,0:T(8,128)} copy(f32[3,4,64,128]{1,0,3,2:T(4,128)} %bitcast.126) | data formatting | bytes 786432 | tf_op jit(solution)/shard_map/all_to_all | solution.py:22
  286.0 2.2 copy.67
  288.1 1.9 copy.68
  290.0 1.8 fusion.37
  291.9 1.8 convolution_convert_fusion
  293.7 1.0 fusion.38
  294.7 1.0 pad_maximum_fusion.7
  295.7 2.6 collective-permute-start.1
  298.3 2.4 collective-permute-done.1
  300.7 6.4 %convolution_bitcast_fusion = f32[128,4096]{1,0:T(8,128)} fusion(bf16[4096,3,256]{2,0,1:T(8,128)(2,1)} %all-gather.3.cloned.1.call-done, f32[130,3,256]{2,0,1:T(8,128)S(1)} %pad_maximum_fusion.6, f32[3,256]{1,0:T(4,128)S(1)} %get-tuple-element.20, f32[3,256]{1,0:T(4,128)S(1)} %get-tuple-element.21, f32[3,256]{1,0:T(4,128)S(1)} %bitcast.136, ...), kind=kOutput, calls=%fused_computation | convolution fusion | flops 806092800 | bytes 9580544 | tf_op jit(solution)/shard_map/dot_general | solution.py:144
  307.2 1.6 convert_element_type.86
  308.7 1.6 fusion.33
  310.3 5.3 %reduce-scatter.2.cloned.1.call-done = bf16[128,1024]{1,0:T(8,128)(2,1)} async-done(((bf16[128,4096]{1,0:T(8,128)(2,1)}), bf16[128,1024]{1,0:T(8,128)(2,1)}) %reduce-scatter.2.cloned.1.call-update) | async-done | bytes 262160 | tf_op jit(solution)/shard_map/reduce_scatter | solution.py:127
  315.6 1.9 add_convert_fusion
  317.5 65.3 %all-reduce.2.cloned.1.call-done = f32[128,4096]{1,0:T(8,128)} async-done(((f32[128,4096]{1,0:T(8,128)}), f32[128,4096]{1,0:T(8,128)}) %all-reduce.2.cloned.1.call-update) | async-done | bytes 2097168 | tf_op jit(solution)/shard_map/psum | solution.py:145
  382.8 2.1 multiply_reduce_fusion
  385.0 1.9 subtract_convert_fusion
  (57 shorter events, 2.9 us)
Async XLA Ops:
  7.2 88.3 %all-gather.3.cloned.1.call-start = ((), (), s32[]{:S(2)}) async-start(), calls=%async_computation.3 | async-start | bytes 6389760 | tf_op jit(solution)/shard_map/all_gather | solution.py:89
  7.9 164.4 %all-gather.5.cloned.1.call-start = ((), (), s32[]{:S(2)}) async-start(), calls=%async_computation.4 | async-start | bytes 2129920 | tf_op jit(solution)/shard_map/all_gather | solution.py:90
  11.6 92.6 %copy-start.13 = (f32[128]{0:T(128)}, f32[128]{0:T(128)S(1)}, u32[]{:S(2)}) copy-start(f32[128]{0:T(128)S(1)} %get-tuple-element.19) | copy-start | bytes 1540
  11.6 92.6 %copy-start = (bf16[128,4096]{1,0:T(8,128)(2,1)S(1)}, bf16[128,4096]{1,0:T(8,128)(2,1)}, u32[]{:S(2)}) copy-start(bf16[128,4096]{1,0:T(8,128)(2,1)} %param.8) | copy-start | bytes 3145732
  11.6 92.6 %copy-start.9 = (f32[4096]{0:T(1024)S(1)}, f32[4096]{0:T(1024)}, u32[]{:S(2)}) copy-start(f32[4096]{0:T(1024)} %param.9) | copy-start | bytes 49156
  104.2 68.1 %copy-start.3 = (bf16[128,4096]{1,0:T(8,128)(2,1)S(1)}, bf16[128,4096]{1,0:T(8,128)(2,1)}, u32[]{:S(2)}) copy-start(bf16[128,4096]{1,0:T(8,128)(2,1)} %param.15) | copy-start | bytes 3145732
  109.3 65.4 %collective-permute-start = (bf16[2,3,256]{2,0,1:T(2,128)(2,1)S(1)}, bf16[2,3,256]{2,0,1:T(2,128)(2,1)S(1)}, u32[]{:S(2)}, u32[]{:S(2)}) collective-permute-start(bf16[2,3,256]{2,0,1:T(2,128)(2,1)S(1)} %bitcast.138), channel_id=1, source_target_pairs={{0,4},{4,8},{8,12},{12,16},{16,20},{20,24},{24,28},{28,32},{32,36}... | collective-permute-start | bytes 9224 | tf_op jit(solution)/shard_map/ppermute | solution.py:14
  174.4 1.0 copy-start.7
  174.4 1.0 copy-start.8
  176.4 23.9 %all-to-all-start = ((f32[3,256,128]{2,0,1:T(4,128)}), f32[3,256,128]{2,0,1:T(4,128)S(1)}, u32[]{:S(2)}, u32[]{:S(2)}) async-start(f32[3,256,128]{2,0,1:T(4,128)} %copy.50), calls=%async_computation | async-start | bytes 1048576 | tf_op jit(solution)/shard_map/all_to_all | solution.py:18
  183.0 132.6 %reduce-scatter.2.cloned.1.call-start = ((), (), s32[]{:S(2)}) async-start(), calls=%async_computation.5 | async-start | bytes 1310720 | tf_op jit(solution)/shard_map/reduce_scatter | solution.py:127
  275.9 14.1 %copy-start.11 = (f32[256]{0:T(256)S(1)}, f32[256]{0:T(256)}, u32[]{:S(2)}) copy-start(f32[256]{0:T(256)} %param.13) | copy-start | bytes 3076
  286.0 5.9 %copy-start.1 = (bf16[256,4096]{0,1:T(8,128)(2,1)S(1)}, bf16[256,4096]{0,1:T(8,128)(2,1)}, u32[]{:S(2)}) copy-start(bf16[256,4096]{0,1:T(8,128)(2,1)} %all-gather.5.cloned.1.call-done) | copy-start | bytes 6291460
  293.6 7.0 %copy-start.5 = (f32[128,1,256]{2,0,1:T(8,128)S(1)}, f32[128,1,256]{2,0,1:T(8,128)}, u32[]{:S(2)}) copy-start(f32[128,1,256]{2,0,1:T(8,128)} %get-tuple-element.5) | copy-start | bytes 393220
  293.6 7.0 %copy-start.6 = (f32[128,1,256]{2,0,1:T(8,128)S(1)}, f32[128,1,256]{2,0,1:T(8,128)}, u32[]{:S(2)}) copy-start(f32[128,1,256]{2,0,1:T(8,128)} %get-tuple-element.13) | copy-start | bytes 393220
  293.7 89.1 %all-reduce.2.cloned.1.call-start = ((), (), s32[]{:S(2)}) async-start(), calls=%async_computation.6 | async-start | bytes 4194304 | tf_op jit(solution)/shard_map/psum | solution.py:145
  295.7 4.9 %collective-permute-start.1 = (f32[2,3,256]{2,0,1:T(2,128)S(1)}, f32[2,3,256]{2,0,1:T(2,128)S(1)}, u32[]{:S(2)}, u32[]{:S(2)}) collective-permute-start(f32[2,3,256]{2,0,1:T(2,128)S(1)} %slice.110), channel_id=1, source_target_pairs={{4,0},{8,4},{12,8},{16,12},{20,16},{24,20},{28,24},{32,28},{36,32}... | collective-permute-start | bytes 18440 | tf_op jit(solution)/shard_map/ppermute | solution.py:14
  307.1 75.6 %copy-start.10 = (f32[4096]{0:T(1024)S(1)}, f32[4096]{0:T(1024)}, u32[]{:S(2)}) copy-start(f32[4096]{0:T(1024)} %param.9) | copy-start | bytes 49156
  310.3 74.6 %copy-start.4 = (bf16[128,4096]{1,0:T(8,128)(2,1)S(1)}, bf16[128,4096]{1,0:T(8,128)(2,1)}, u32[]{:S(2)}) copy-start(bf16[128,4096]{1,0:T(8,128)(2,1)} %param.15) | copy-start | bytes 3145732
  310.3 74.6 %copy-start.12 = (f32[128]{0:T(128)S(1)}, f32[128]{0:T(128)}, u32[]{:S(2)}) copy-start(f32[128]{0:T(128)} %get-tuple-element.18) | copy-start | bytes 1540
  310.3 74.6 %copy-start.14 = (f32[128]{0:T(128)S(1)}, f32[128]{0:T(128)}, u32[]{:S(2)}) copy-start(f32[128]{0:T(128)} %copy-done.13) | copy-start | bytes 1540
  382.8 2.2 copy-start.2
Sparse Core Ops, SparseCore 0:
  10.8 84.6 all-gather.2
  98.3 74.0 all-gather.4
  293.8 21.7 reduce-scatter.1
  317.8 64.9 all-reduce.1
where the time goes:
time: 395 us; the launch traced here: 393 us
  waiting for transfers between devices  235 us (59%)
  local copies, waits for them, and re-layouts  62.4 us (16%)
  matrix products  31.7 us (8%)
  blocking collectives  20.6 us (5%)
  other arithmetic  17.5 us (4%)
  between operations  14.1 us (4%)
  starting transfers between devices  12.2 us (3%)
    all_gather x1, waiting for transfers between devices, per_device(): lax.all_gather(in_weight, 'seq', axis=0, tiled=True)  83.9 us
    psum x1, waiting for transfers between devices, per_device(): norm_grad = lax.psum(partial_grad, 'ch')  65.3 us
    all_gather x1, waiting for transfers between devices, per_device(): lax.all_gather(out_weight, 'seq', axis=1, tiled=True)  60.2 us
    unnamed x34, local copies, waits for them, and re-layouts  28.1 us
    all_to_all x1, blocking collectives, to_rows(): lax.all_to_all(signals, 'seq', split_axis=2, concat_axis=1, tiled=True)  20.6 us
    all_to_all x1, waiting for transfers between devices, to_columns(): lax.all_to_all(signals, 'seq', split_axis=1, concat_axis=2, tiled=True)  16.3 us
    all_to_all x4, local copies, waits for them, and re-layouts, to_rows(): lax.all_to_all(signals, 'seq', split_axis=2, concat_axis=1, tiled=True)  14.6 us
    all_gather x1, local copies, waits for them, and re-layouts, per_device(): lax.all_gather(in_weight, 'seq', axis=0, tiled=True)  8.7 us
  transfers between devices with their start and end apart: 7, of which 6 were waited for; matrix products, arithmetic and copies ran while one was open for 8% of the time, Pallas kernels for 0%

commit v1 on v0

--- a/solution.py
+++ b/solution.py
@@ -19,7 +19,10 @@
 
 
 def to_rows(signals):
-    return lax.all_to_all(signals, "seq", split_axis=2, concat_axis=1, tiled=True)
+    return jnp.concatenate(
+        lax.all_to_all(jnp.stack(jnp.split(signals, lax.axis_size("seq"), axis=2)), "seq", 0, 0),
+        axis=1,
+    )
 
 
 def turn_table(rows, cols, period, sign):

time: 395 us -> 376 us (0.952)
  local copies, waits for them, and re-layouts: 62.4 us -> 44.6 us
    all_to_all x4 -> x0, local copies, waits for them, and re-layouts: 14.6 us -> none  [to_rows(): lax.all_to_all(signals, 'seq', split_axis=2, concat_axis=1, tiled=True)]
    div x1, local copies, waits for them, and re-layouts: 8.64 us -> 0.15 us  [inverse_dft(): return grid.reshape(count, chans, outer * inner // 2) / float(outer * inner)]
    unnamed x34 -> x97, local copies, waits for them, and re-layouts: 28.1 us -> 30 us
  transfers between devices with their start and end apart: 7 -> 7, of which waited for: 6 -> 6; matrix products, arithmetic and copies ran while one was open for 8% -> 9% of each run, Pallas kernels for 0% -> 0%
where the time goes in v1:
time: 376 us; the launch traced here: 374 us
  waiting for transfers between devices  235 us (62%)
  local copies, waits for them, and re-layouts  44.6 us (12%)
  matrix products  31.8 us (8%)
  blocking collectives  20.6 us (5%)
  other arithmetic  15.8 us (4%)
  between operations  14.2 us (4%)
  starting transfers between devices  12 us (3%)
    all_gather x1, waiting for transfers between devices, per_device(): lax.all_gather(in_weight, 'seq', axis=0, tiled=True)  83.9 us
    psum x1, waiting for transfers between devices, per_device(): norm_grad = lax.psum(partial_grad, 'ch')  65.4 us
    all_gather x1, waiting for transfers between devices, per_device(): lax.all_gather(out_weight, 'seq', axis=1, tiled=True)  60.2 us
    unnamed x97, local copies, waits for them, and re-layouts  30 us
    all_to_all x1, blocking collectives, to_rows(): lax.all_to_all(jnp.stack(jnp.split(signals, lax.axis_size('seq'), axis=2)...  20.6 us
    all_to_all x1, waiting for transfers between devices, to_columns(): lax.all_to_all(signals, 'seq', split_axis=1, concat_axis=2, tiled=True)  16.3 us
    all_gather x1, local copies, waits for them, and re-layouts, per_device(): lax.all_gather(in_weight, 'seq', axis=0, tiled=True)  8.72 us
  transfers between devices with their start and end apart: 7, of which 6 were waited for; matrix products, arithmetic and copies ran while one was open for 9% of the time, Pallas kernels for 0%

profile of v1, /device:TPU:1, one launch (start us, length us, event | category | flops | bytes accessed | tf_op | source)
XLA Modules:
  0.0 374.2 jit_solution(1003825920578293716)
XLA Ops:
  8.6 0.8 fusion.142
  9.5 1.5 multiply_reduce_fusion.1
  11.6 83.9 %all-gather.3.cloned.1.call-done = bf16[4096,3,256]{2,0,1:T(8,128)(2,1)} async-done(((bf16[64,3,256]{2,0,1:T(8,128)(2,1)}), bf16[4096,3,256]{2,0,1:T(8,128)(2,1)}) %all-gather.3.cloned.1.call-update) | async-done | bytes 6291472 | tf_op jit(solution)/shard_map/all_gather | solution.py:92
  95.5 8.7 %copy.172 = bf16[4096,3,256]{0,2,1:T(8,128)(2,1)} copy(bf16[4096,3,256]{2,0,1:T(8,128)(2,1)} %all-gather.3.cloned.1.call-done) | data formatting | bytes 12582912 | tf_op jit(solution)/shard_map/all_gather | solution.py:92
  104.2 5.1 %convolution_convert_fusion.1 = bf16[128,768]{1,0:T(8,128)(2,1)S(1)} fusion(bf16[4096,768]{0,1:T(8,128)(2,1)} %bitcast.379, bf16[128,4096]{1,0:T(8,128)(2,1)S(1)} %copy-done, f32[4096]{0:T(1024)S(1)} %copy-done.10, f32[128]{0:T(128)S(1)} %get-tuple-element.19), kind=kOutput, calls=%fused_computation.16 | convolution fusion | flops 807501824 | bytes 7553536 | tf_op jit(solution)/shard_map/dot_general | solution.py:96
  109.4 2.7 collective-permute-start
  112.1 60.2 %all-gather.5.cloned.1.call-done = bf16[256,4096]{0,1:T(8,128)(2,1)} async-done(((bf16[256,64]{0,1:T(8,128)(2,1)}), bf16[256,4096]{0,1:T(8,128)(2,1)}) %all-gather.5.cloned.1.call-update) | async-done | bytes 2097168 | tf_op jit(solution)/shard_map/all_gather | solution.py:93
  172.3 2.0 fusion.143
  175.4 1.0 copy.176
  176.4 6.6 %all-to-all-start = ((f32[3,256,128]{2,0,1:T(4,128)}), f32[3,256,128]{2,0,1:T(4,128)S(1)}, u32[]{:S(2)}, u32[]{:S(2)}) async-start(f32[3,256,128]{2,0,1:T(4,128)} %copy.176), calls=%async_computation | async-start | bytes 1048576 | tf_op jit(solution)/shard_map/all_to_all | solution.py:18
  183.9 16.3 %all-to-all-done = f32[3,256,128]{2,0,1:T(4,128)S(1)} async-done(((f32[3,256,128]{2,0,1:T(4,128)}), f32[3,256,128]{2,0,1:T(4,128)S(1)}, u32[]{:S(2)}, u32[]{:S(2)}) %all-to-all-start) | async-done | bytes 393248 | tf_op jit(solution)/shard_map/all_to_all | solution.py:18
  200.3 1.5 convolution_bitcast_fusion.1
  201.8 1.5 fusion
  203.3 1.6 fusion.31
  204.9 1.6 fusion.32
  206.5 1.6 convolution_add_fusion.1
  208.1 1.6 convolution_subtract_fusion.1
  209.9 1.1 fusion.13
  211.0 1.3 fusion.12
  212.4 1.1 convolution_subtract_fusion
  213.5 1.1 convolution_add_fusion
  214.6 1.2 fusion.8
  215.8 1.2 fusion.2
  217.9 0.8 constant_dynamic-update-slice_fusion.41
  218.7 0.7 constant_dynamic-update-slice_fusion.40
  222.9 0.7 constant_dynamic-update-slice_fusion.34
  223.6 0.7 constant_dynamic-update-slice_fusion.33
  224.3 0.7 constant_dynamic-update-slice_fusion.32
  239.7 0.7 constant_dynamic-update-slice_fusion.10
  242.5 0.7 constant_dynamic-update-slice_fusion.6
  246.7 0.7 constant_dynamic-update-slice_fusion
  247.4 20.6 %all_to_all.20 = f32[64,3,4,128]{3,2,1,0:T(4,128)S(1)} all-to-all(f32[64,3,4,128]{3,2,1,0:T(4,128)S(1)} %constant_dynamic-update-slice_fusion), channel_id=1, replica_groups=mesh['seq'=64,'ch'=4] {'seq'}, dimensions={0} | all-to-all | bytes 786432 | tf_op jit(solution)/shard_map/all_to_all | solution.py:23
  268.0 0.8 copy.191
  268.8 1.9 copy.192
  270.8 1.8 fusion.37
  272.6 1.8 convolution_convert_fusion
  274.5 1.0 fusion.38
  275.4 1.0 pad_maximum_fusion.7
  276.5 2.3 collective-permute-start.1
  278.8 2.6 collective-permute-done.1
  281.4 6.5 %convolution_bitcast_fusion = f32[128,4096]{1,0:T(8,128)} fusion(bf16[4096,3,256]{2,0,1:T(8,128)(2,1)} %all-gather.3.cloned.1.call-done, f32[130,3,256]{2,0,1:T(8,128)S(1)} %pad_maximum_fusion.6, f32[3,256]{1,0:T(4,128)S(1)} %get-tuple-element.20, f32[3,256]{1,0:T(4,128)S(1)} %get-tuple-element.21, f32[3,256]{1,0:T(4,128)S(1)} %bitcast.388, ...), kind=kOutput, calls=%fused_computation | convolution fusion | flops 806092800 | bytes 9580544 | tf_op jit(solution)/shard_map/dot_general | solution.py:147
  288.0 1.5 convert_element_type.86
  289.5 1.6 fusion.33
  291.1 5.2 %reduce-scatter.2.cloned.1.call-done = bf16[128,1024]{1,0:T(8,128)(2,1)} async-done(((bf16[128,4096]{1,0:T(8,128)(2,1)}), bf16[128,1024]{1,0:T(8,128)(2,1)}) %reduce-scatter.2.cloned.1.call-update) | async-done | bytes 262160 | tf_op jit(solution)/shard_map/reduce_scatter | solution.py:130
  296.3 1.9 add_convert_fusion
  298.1 65.4 %all-reduce.2.cloned.1.call-done = f32[128,4096]{1,0:T(8,128)} async-done(((f32[128,4096]{1,0:T(8,128)}), f32[128,4096]{1,0:T(8,128)}) %all-reduce.2.cloned.1.call-update) | async-done | bytes 2097168 | tf_op jit(solution)/shard_map/psum | solution.py:148
  363.5 2.1 multiply_reduce_fusion
  365.7 1.9 subtract_convert_fusion
  (118 shorter events, 28.9 us)
Async XLA Ops:
  7.2 88.3 %all-gather.3.cloned.1.call-start = ((), (), s32[]{:S(2)}) async-start(), calls=%async_computation.3 | async-start | bytes 6389760 | tf_op jit(solution)/shard_map/all_gather | solution.py:92
  7.9 164.4 %all-gather.5.cloned.1.call-start = ((), (), s32[]{:S(2)}) async-start(), calls=%async_computation.4 | async-start | bytes 2129920 | tf_op jit(solution)/shard_map/all_gather | solution.py:93
  11.6 92.7 %copy-start.14 = (f32[128]{0:T(128)}, f32[128]{0:T(128)S(1)}, u32[]{:S(2)}) copy-start(f32[128]{0:T(128)S(1)} %get-tuple-element.19) | copy-start | bytes 1540
  11.6 92.7 %copy-start = (bf16[128,4096]{1,0:T(8,128)(2,1)S(1)}, bf16[128,4096]{1,0:T(8,128)(2,1)}, u32[]{:S(2)}) copy-start(bf16[128,4096]{1,0:T(8,128)(2,1)} %param.8) | copy-start | bytes 3145732
  11.6 92.7 %copy-start.10 = (f32[4096]{0:T(1024)S(1)}, f32[4096]{0:T(1024)}, u32[]{:S(2)}) copy-start(f32[4096]{0:T(1024)} %param.9) | copy-start | bytes 49156
  104.2 68.1 %copy-start.3 = (bf16[128,4096]{1,0:T(8,128)(2,1)S(1)}, bf16[128,4096]{1,0:T(8,128)(2,1)}, u32[]{:S(2)}) copy-start(bf16[128,4096]{1,0:T(8,128)(2,1)} %param.15) | copy-start | bytes 3145732
  109.4 65.4 %collective-permute-start = (bf16[2,3,256]{2,0,1:T(2,128)(2,1)S(1)}, bf16[2,3,256]{2,0,1:T(2,128)(2,1)S(1)}, u32[]{:S(2)}, u32[]{:S(2)}) collective-permute-start(bf16[2,3,256]{2,0,1:T(2,128)(2,1)S(1)} %bitcast.390), channel_id=1, source_target_pairs={{0,4},{4,8},{8,12},{12,16},{16,20},{20,24},{24,28},{28,32},{32,36}... | collective-permute-start | bytes 9224 | tf_op jit(solution)/shard_map/ppermute | solution.py:14
  174.4 1.0 copy-start.8
  174.4 1.0 copy-start.9
  176.4 23.9 %all-to-all-start = ((f32[3,256,128]{2,0,1:T(4,128)}), f32[3,256,128]{2,0,1:T(4,128)S(1)}, u32[]{:S(2)}, u32[]{:S(2)}) async-start(f32[3,256,128]{2,0,1:T(4,128)} %copy.176), calls=%async_computation | async-start | bytes 1048576 | tf_op jit(solution)/shard_map/all_to_all | solution.py:18
  183.0 113.3 %reduce-scatter.2.cloned.1.call-start = ((), (), s32[]{:S(2)}) async-start(), calls=%async_computation.5 | async-start | bytes 1310720 | tf_op jit(solution)/shard_map/reduce_scatter | solution.py:130
  217.0 53.8 %copy-start.12 = (f32[256]{0:T(256)S(1)}, f32[256]{0:T(256)}, u32[]{:S(2)}) copy-start(f32[256]{0:T(256)} %param.13) | copy-start | bytes 3076
  217.1 0.7 copy-start.7
  217.9 54.7 %copy-start.1 = (bf16[256,4096]{0,1:T(8,128)(2,1)S(1)}, bf16[256,4096]{0,1:T(8,128)(2,1)}, u32[]{:S(2)}) copy-start(bf16[256,4096]{0,1:T(8,128)(2,1)} %all-gather.5.cloned.1.call-done) | copy-start | bytes 6291460
  274.4 7.0 %copy-start.5 = (f32[128,1,256]{2,0,1:T(8,128)S(1)}, f32[128,1,256]{2,0,1:T(8,128)}, u32[]{:S(2)}) copy-start(f32[128,1,256]{2,0,1:T(8,128)} %get-tuple-element.5) | copy-start | bytes 393220
  274.4 7.0 %copy-start.6 = (f32[128,1,256]{2,0,1:T(8,128)S(1)}, f32[128,1,256]{2,0,1:T(8,128)}, u32[]{:S(2)}) copy-start(f32[128,1,256]{2,0,1:T(8,128)} %get-tuple-element.13) | copy-start | bytes 393220
  274.4 89.1 %all-reduce.2.cloned.1.call-start = ((), (), s32[]{:S(2)}) async-start(), calls=%async_computation.6 | async-start | bytes 4194304 | tf_op jit(solution)/shard_map/psum | solution.py:148
  276.5 4.9 %collective-permute-start.1 = (f32[2,3,256]{2,0,1:T(2,128)S(1)}, f32[2,3,256]{2,0,1:T(2,128)S(1)}, u32[]{:S(2)}, u32[]{:S(2)}) collective-permute-start(f32[2,3,256]{2,0,1:T(2,128)S(1)} %slice.110), channel_id=1, source_target_pairs={{4,0},{8,4},{12,8},{16,12},{20,16},{24,20},{28,24},{32,28},{36,32}... | collective-permute-start | bytes 18440 | tf_op jit(solution)/shard_map/ppermute | solution.py:14
  288.0 75.5 %copy-start.11 = (f32[4096]{0:T(1024)S(1)}, f32[4096]{0:T(1024)}, u32[]{:S(2)}) copy-start(f32[4096]{0:T(1024)} %param.9) | copy-start | bytes 49156
  291.1 74.5 %copy-start.4 = (bf16[128,4096]{1,0:T(8,128)(2,1)S(1)}, bf16[128,4096]{1,0:T(8,128)(2,1)}, u32[]{:S(2)}) copy-start(bf16[128,4096]{1,0:T(8,128)(2,1)} %param.15) | copy-start | bytes 3145732
  291.1 74.5 %copy-start.13 = (f32[128]{0:T(128)S(1)}, f32[128]{0:T(128)}, u32[]{:S(2)}) copy-start(f32[128]{0:T(128)} %get-tuple-element.18) | copy-start | bytes 1540
  291.1 74.5 %copy-start.15 = (f32[128]{0:T(128)S(1)}, f32[128]{0:T(128)}, u32[]{:S(2)}) copy-start(f32[128]{0:T(128)} %copy-done.14) | copy-start | bytes 1540
  363.5 2.2 copy-start.2
Sparse Core Ops, SparseCore 0:
  10.8 84.6 all-gather.2
  98.3 74.0 all-gather.4
  274.5 21.6 reduce-scatter.1
  298.5 64.9 all-reduce.1
